TPU v7x, 512 devices: a whole 4x8x8 slice. The times are simulated.
512 devices in a mesh: dp: 4 (over z_lo, core), ctx: 128 (over x, y, z_hi).
Axes of the slice: x: 4, y: 8, z: 8 (z_hi: 4, z_lo: 2; z = z_hi * 2 + z_lo), core: 2. Of those that a mesh axis runs over, the one named last changes fastest.
Arguments:
- query: bfloat16 [4, 32768, 1024], P('dp', 'ctx'), may hold values from -150 to 150
- key: bfloat16 [4, 32768, 1024], P('dp', 'ctx'), may hold values from -3 to 3
- value: bfloat16 [4, 32768, 1024], P('dp', 'ctx'), may hold values from -6 to 6
- grad_out: bfloat16 [4, 32768, 1024], P('dp', 'ctx'), may hold values from -30 to 30
- clause: int32 [4, 32768], P('dp', 'ctx'), may hold values from 0 to 2047, never falling along the last dimension, each value on 1 to 48 neighbouring positions
- bias_table: float32 [32, 2], replicated, may hold values from -1.5 to 1.5
Outputs:
- attended: bfloat16 [4, 32768, 1024], P('dp', 'ctx')
- query_gradient: bfloat16 [4, 32768, 1024], P('dp', 'ctx')
- key_gradient: bfloat16 [4, 32768, 1024], P('dp', 'ctx')
- value_gradient: bfloat16 [4, 32768, 1024], P('dp', 'ctx')
- bias_grad: float32 [32, 2], replicated
Inputs may be any that keep to these rules, and one draw needn't show every extreme that they name: Clause ids never fall along a document; a clause holds 1 to 48 tokens, and some clause holds exactly 48.
All inputs are finite; a program needn't handle non-finite values.
Results may differ from a plain program's by a relative error of at most 0.009.
Values may be sent and summed in bfloat16 or wider, within the bound.
No kernel may reach another device: no remote copies, remote signals or barrier semaphores. Data moves between devices by JAX's collectives and lax.ppermute only.
A program may use at most 128 MiB of HBM per device.

v0:
```python
import jax
import jax.numpy as jnp
from jax import lax
from jax.sharding import Mesh, PartitionSpec as P

HEADS = 8
WINDOW = 512
BUCKETS = 32
DILATION_FIRST = 1
DILATION_SECOND = 8
DILATION_THIRD = 32
CTX = ("cx", "cy", "cz")


def swapped(block, axis, bit):
    count = lax.axis_size(axis)
    route = []
    for low in range(count):
        high = low | 1 << bit
        if high != low and high < count:
            route += [(low, high), (high, low)]
    return lax.ppermute(block, axis, route)


def shifted(value, axis, steps):
    count = lax.axis_size(axis)
    leading, last = (max(0, -steps), min(count, count - steps))
    return lax.ppermute(value, axis, [(source, source + steps) for source in range(leading, last)])


def with_halo(shard, sides, width):
    for axis, dim in sides:
        size, length = (lax.axis_size(axis), shard.shape[dim])
        up = [(i, (i + 1) % size) for i in range(size - 1)]
        down = [(j, i) for i, j in up]
        last = lax.slice_in_dim(shard, length - width, length, axis=dim)
        leading = lax.slice_in_dim(shard, 0, width, axis=dim)
        before = lax.ppermute(last, axis, up)
        after = lax.ppermute(leading, axis, down)
        shard = jnp.concatenate([before, shard, after], axis=dim)
    return shard


def sample_rows(matrix, initial_flag, dilation_rate):
    count = matrix.shape[0] // dilation_rate
    head_dim = matrix.shape[1] // HEADS
    grid = matrix.reshape(count, dilation_rate, HEADS, head_dim)
    return jnp.concatenate(
        [grid[:, 0, initial_flag], grid[:, dilation_rate // 2, initial_flag + 1]], axis=1
    )


def spread_rows(sampled, dilation_rate):
    count = sampled.shape[0]
    grid = jnp.zeros((count, dilation_rate) + sampled.shape[1:], sampled.dtype)
    grid = grid.at[:, 0, 0].set(sampled[:, 0]).at[:, dilation_rate // 2, 1].set(sampled[:, 1])
    return grid.reshape((count * dilation_rate,) + sampled.shape[1:])


def upper_half(bit):
    index = lax.axis_index(CTX)
    return index // 2**bit % 2 == 1


def double_rows(block, bits):
    for bit in range(bits):
        other = swapped(block, CTX, bit)
        block = jnp.where(
            upper_half(bit),
            jnp.concatenate([other, block], axis=0),
            jnp.concatenate([block, other], axis=0),
        )
    return block


def halve_sums(block, bits):
    for bit in reversed(range(bits)):
        half = block.shape[0] // 2
        lower, higher = (block[:half], block[half:])
        upper = upper_half(bit)
        outgoing = jnp.where(upper, lower, higher)
        staying = jnp.where(upper, higher, lower)
        block = staying + swapped(outgoing.astype(jnp.bfloat16), CTX, bit).astype(outgoing.dtype)
    return block


def span_rows(block, bits):
    return double_rows(block, bits)


def span_sums(block, bits):
    return halve_sums(block, bits)


def rows_side(score_matrix, every_key_rows, every_value_rows, gradient_list, score_scale):
    top = jnp.max(score_matrix, axis=-1, keepdims=True)
    raised = jnp.exp(score_matrix - top)
    totals = jnp.sum(raised, axis=-1, keepdims=True)
    shares = raised / totals
    softmax_weights = shares.astype(jnp.bfloat16)
    attended = jnp.einsum(
        "ezb,beo->zeo", softmax_weights, every_value_rows, preferred_element_type=jnp.float32
    )
    weight_gradient = jnp.einsum(
        "wvx,yvx->vwy", gradient_list, every_value_rows, preferred_element_type=jnp.float32
    )
    delta = jnp.sum(shares * weight_gradient, axis=-1, keepdims=True)
    logit_grads = shares * (weight_gradient - delta)
    score_gradient = logit_grads.astype(jnp.bfloat16)
    query_gradient = (
        jnp.einsum(
            "ezb,beo->zeo", score_gradient, every_key_rows, preferred_element_type=jnp.float32
        )
        * score_scale
    )
    return (
        attended,
        query_gradient,
        softmax_weights,
        score_gradient,
        logit_grads,
        top,
        totals,
        delta,
    )


def keys_side(softmax_weights, score_gradient, query_matrix, gradient_list, score_scale):
    key_gradient = (
        jnp.einsum("vjb,jvw->bvw", score_gradient, query_matrix, preferred_element_type=jnp.float32)
        * score_scale
    )
    value_gradient = jnp.einsum(
        "vjb,jvw->bvw", softmax_weights, gradient_list, preferred_element_type=jnp.float32
    )
    return (key_gradient, value_gradient)


def bucket_lookup(bucket, table):
    running = jnp.zeros((table.shape[1],) + bucket.shape, jnp.float32)
    for level in range(BUCKETS):
        running = jnp.where(bucket[None] == level, table[level][:, None, None], running)
    return running


def bucket_sums(bucket, logit_grads):
    totals = [
        jnp.sum(jnp.where(bucket[None] == level, logit_grads, 0.0), axis=(1, 2))
        for level in range(BUCKETS)
    ]
    return jnp.stack(totals, axis=0)


def pass_rim(rim, offset):
    return shifted(rim.astype(jnp.bfloat16), CTX, offset).astype(rim.dtype)


def band_part(query_rows, key_rows, value_rows, grad_rows, clause_rows, table, score_scale):
    rows, width = query_rows.shape
    head_dim = width // HEADS
    wide = 2 * head_dim
    half = WINDOW // 2
    pair_rows = jnp.concatenate([key_rows[:, :wide], value_rows[:, :wide]], axis=1)
    extended, extended_clause = (
        with_halo(pair_rows, ((CTX, 0),), half),
        with_halo(clause_rows, ((CTX, 0),), half),
    )
    reach = rows + 2 * half
    nearby_key_rows = extended[:, :wide].reshape(reach, 2, head_dim)
    values_near = extended[:, wide:].reshape(reach, 2, head_dim)
    query_matrix = query_rows[:, :wide].reshape(rows, 2, head_dim)
    gradient_list = grad_rows[:, :wide].reshape(rows, 2, head_dim)
    start = lax.axis_index(CTX) * rows
    length = rows * lax.axis_size(CTX)
    local_query = jnp.arange(rows)[:, None]
    local_key = jnp.arange(reach)[None, :] - half
    global_key = start + local_key
    allowed = (jnp.abs(local_query - local_key) < half) & (global_key >= 0) & (global_key < length)
    bucket = jnp.minimum(jnp.abs(clause_rows[:, None] - extended_clause[None, :]), BUCKETS - 1)
    score_matrix = (
        jnp.einsum(
            "wvx,yvx->vwy", query_matrix, nearby_key_rows, preferred_element_type=jnp.float32
        )
        * score_scale
    )
    score_matrix = jnp.where(allowed[None], score_matrix + bucket_lookup(bucket, table), -jnp.inf)
    attended, query_gradient, softmax_weights, score_gradient, logit_grads, top, totals, delta = (
        rows_side(score_matrix, nearby_key_rows, values_near, gradient_list, score_scale)
    )
    key_gradient, value_gradient = keys_side(
        softmax_weights, score_gradient, query_matrix, gradient_list, score_scale
    )
    sums = jnp.concatenate(
        [key_gradient.reshape(reach, wide), value_gradient.reshape(reach, wide)], axis=1
    )
    own = sums[half : half + rows]
    from_next = pass_rim(sums[:half], -1)
    from_prev = pass_rim(sums[half + rows :], 1)
    own = own.at[rows - half :].add(from_next).at[:half].add(from_prev)
    own_key = own[:, :wide].reshape(rows, 2, head_dim)
    own_value = own[:, wide:].reshape(rows, 2, head_dim)
    return (attended, query_gradient, own_key, own_value, bucket_sums(bucket, logit_grads))


def dilated(
    query_rows, key_rows, value_rows, grad_rows, initial_flag, dilation_rate, bits, score_scale
):
    head_dim = query_rows.shape[1] // HEADS
    wide = 2 * head_dim
    picked_query = sample_rows(query_rows, initial_flag, dilation_rate)
    picked_key = sample_rows(key_rows, initial_flag, dilation_rate)
    picked_value = sample_rows(value_rows, initial_flag, dilation_rate)
    picked_grad = sample_rows(grad_rows, initial_flag, dilation_rate)
    count = picked_query.shape[0]
    gathered = lax.all_gather(
        jnp.concatenate([picked_key, picked_value], axis=1), bits, axis=0, tiled=True
    )
    gathered_rows = gathered.shape[0]
    every_key_rows = gathered[:, :wide].reshape(gathered_rows, 2, head_dim)
    every_value_rows = gathered[:, wide:].reshape(gathered_rows, 2, head_dim)
    query_matrix = picked_query.reshape(count, 2, head_dim)
    gradient_list = picked_grad.reshape(count, 2, head_dim)
    score_matrix = (
        jnp.einsum("wvx,yvx->vwy", query_matrix, every_key_rows, preferred_element_type=jnp.float32)
        * score_scale
    )
    attended, query_gradient, softmax_weights, score_gradient, logit_grads, top, totals, delta = (
        rows_side(score_matrix, every_key_rows, every_value_rows, gradient_list, score_scale)
    )
    key_gradient, value_gradient = keys_side(
        softmax_weights, score_gradient, query_matrix, gradient_list, score_scale
    )
    partial_sums = jnp.concatenate(
        [key_gradient.reshape(gathered_rows, wide), value_gradient.reshape(gathered_rows, wide)],
        axis=1,
    )
    own = lax.psum_scatter(partial_sums, bits, scatter_dimension=0, tiled=True)
    own_key = own[:, :wide].reshape(count, 2, head_dim)
    own_value = own[:, wide:].reshape(count, 2, head_dim)
    return (
        spread_rows(attended, dilation_rate),
        spread_rows(query_gradient, dilation_rate),
        spread_rows(own_key, dilation_rate),
        spread_rows(own_value, dilation_rate),
    )


def shards(query, key, value, grad_out, clause, bias_table):
    query_rows = query[0]
    key_rows = key[0]
    value_rows = value[0]
    grad_rows = grad_out[0]
    clause_rows = clause[0]
    rows, width = query_rows.shape
    head_dim = width // HEADS
    score_scale = head_dim ** (-0.5)
    band = band_part(
        query_rows, key_rows, value_rows, grad_rows, clause_rows, bias_table, score_scale
    )
    pieces = [band[:4]]
    for initial_flag, dilation_rate, bits in (
        (2, DILATION_FIRST, CTX[2:]),
        (4, DILATION_SECOND, CTX[1:]),
        (6, DILATION_THIRD, CTX),
    ):
        pieces.append(
            dilated(
                query_rows,
                key_rows,
                value_rows,
                grad_rows,
                initial_flag,
                dilation_rate,
                bits,
                score_scale,
            )
        )
    bias_grad = lax.psum(band[4], ("dp",) + CTX)
    joined = [
        jnp.concatenate([piece[slot] for piece in pieces], axis=1)
        .reshape(1, rows, width)
        .astype(jnp.bfloat16)
        for slot in range(4)
    ]
    return (joined[0], joined[1], joined[2], joined[3], bias_grad)


def solution(mesh):
    ctx_size = mesh.shape["ctx"]
    parts = (4, 8, ctx_size // 32)
    split = Mesh(mesh.devices.reshape((mesh.shape["dp"],) + parts), ("dp",) + CTX)
    in_specs = (
        P("dp", CTX, None),
        P("dp", CTX, None),
        P("dp", CTX, None),
        P("dp", CTX, None),
        P("dp", CTX),
        P(),
    )
    out_specs = (
        P("dp", CTX, None),
        P("dp", CTX, None),
        P("dp", CTX, None),
        P("dp", CTX, None),
        P(),
    )
    return jax.shard_map(
        shards, mesh=split, in_specs=in_specs, out_specs=out_specs, check_vma=False
    )
```

profile of v0, /device:TPU:64, one launch (start us, length us, event | category | flops | bytes accessed | tf_op | source)
XLA Modules:
  0.0 1330.2 jit_solution(18316485275672854321)
XLA Ops:
  13.0 6.7 collective-permute-start.2
  21.8 7.8 collective-permute-start
  34.0 1.4 fusion.55
  40.6 5.3 fusion.53
  46.3 5.0 collective-permute-done
  53.0 5.7 fusion.9
  60.4 5.5 select_reduce_fusion
  65.9 4.6 all-gather.4.cloned.1.call-done
  71.8 3.7 fusion.132
  75.5 3.2 fusion.60
  78.7 2.3 multiply_reduce_fusion
  83.2 1.5 pad_maximum_fusion
  84.7 5.4 select_reduce_fusion.18
  92.8 1.3 copy.583
  94.1 1.3 copy.584
  109.3 1.4 copy.589
  123.2 1.3 copy.576
  127.1 1.3 copy.573
  130.9 3.4 fusion.65
  137.9 6.2 collective-permute-start.5
  145.2 103.3 %psum.7 = f32[32,2]{0,1:T(2,128)} all-reduce(f32[32,2]{0,1:T(2,128)S(1)} %stack.131), channel_id=1, replica_groups=mesh['dp'=4,'cx'=4,'cy'=8,'cz'=4] {'dp','cx','cy','cz'}, use_global_device_ids=true, to_apply=%region_47.48 | all-reduce | flops 64 | bytes 512 | tf_op jit(solution)/shard_map/psum | solution.py:278
  248.4 3.2 fusion.15
  251.6 2.0 fusion.16
  255.7 2.0 convolution_bitcast_fusion
  260.4 1.4 fusion.71
  263.1 1.8 copy.629
  268.9 6.5 all-gather.8.cloned.1.call-done
  278.3 1.3 fusion.77
  281.0 1.9 copy.631
  286.6 38.0 %reduce-scatter.8.cloned.1.call-done = f32[256,512]{0,1:T(8,128)} async-done(((f32[1024,512]{0,1:T(8,128)}), f32[256,512]{0,1:T(8,128)}) %reduce-scatter.8.cloned.1.call-update) | async-done | bytes 524304 | tf_op jit(solution)/shard_map/reduce_scatter | solution.py:237
  327.1 233.6 %reduce-scatter.10.cloned.1.call-done = f32[32,512]{1,0:T(8,128)} async-done(((f32[1024,512]{1,0:T(8,128)}), f32[32,512]{1,0:T(8,128)}) %reduce-scatter.10.cloned.1.call-update) | async-done | bytes 65552
  562.5 757.5 %reduce-scatter.12.cloned.1.call-done = f32[8,512]{1,0:T(8,128)} async-done(((f32[1024,512]{1,0:T(8,128)}), f32[8,512]{1,0:T(8,128)}) %reduce-scatter.12.cloned.1.call-update) | async-done | bytes 16400 | tf_op jit(solution)/shard_map/reduce_scatter | solution.py:237
  (449 shorter events, 87.0 us)
Async XLA Ops:
  7.2 63.3 %all-gather.4.cloned.1.call-start = ((), (), s32[]{:S(2)}) async-start(), calls=%async_computation.3 | async-start | bytes 1310720 | tf_op jit(solution)/shard_map/all_gather | solution.py:215
  10.6 247.0 %all-gather.6.cloned.1.call-start = ((), (), s32[]{:S(2)}) async-start(), calls=%async_computation.4 | async-start | bytes 1081344 | tf_op jit(solution)/shard_map/all_gather | solution.py:215
  10.7 19.7 %copy-start.16 = (f32[32,2]{0,1:T(2,128)S(1)}, f32[32,2]{0,1:T(2,128)}, u32[]{:S(2)}) copy-start(f32[32,2]{0,1:T(2,128)} %param.67) | copy-start | bytes 772
  10.8 20.6 %copy-start.9 = (bf16[1,256,1024]{2,1,0:T(8,128)(2,1)S(1)}, bf16[1,256,1024]{2,1,0:T(8,128)(2,1)}, u32[]{:S(2)}) copy-start(bf16[1,256,1024]{2,1,0:T(8,128)(2,1)} %param.65) | copy-start | bytes 1572868
  11.7 263.7 %all-gather.8.cloned.1.call-start = ((), (), s32[]{:S(2)}) async-start(), calls=%async_computation.5 | async-start | bytes 1056768 | tf_op jit(solution)/shard_map/all_gather | solution.py:215
  11.7 28.8 %collective-permute-start.3 = (s32[256]{0:T(256)S(1)}, s32[256]{0:T(256)S(1)}, u32[]{:S(2)}, u32[]{:S(2)}) collective-permute-start(s32[256]{0:T(256)S(1)} %bitcast.406), channel_id=1, source_target_pairs={{1,0},{2,1},{3,2},{4,3},{5,4},{6,5},{7,6},{8,7},{9,8},{10,9},{11,1... | collective-permute-start | bytes 3080 | tf_op jit(solution)/shard_map/ppermute | solution.py:39
  13.0 27.6 %collective-permute-start.2 = (s32[256]{0:T(256)S(1)}, s32[256]{0:T(256)S(1)}, u32[]{:S(2)}, u32[]{:S(2)}) collective-permute-start(s32[256]{0:T(256)S(1)} %bitcast.407), channel_id=1, source_target_pairs={{0,1},{1,2},{2,3},{3,4},{4,5},{5,6},{6,7},{7,8},{8,9},{9,10},{10,1... | collective-permute-start | bytes 3080 | tf_op jit(solution)/shard_map/ppermute | solution.py:38
  19.8 12.0 copy-start.10
  20.5 25.8 %collective-permute-start.1 = (bf16[256,512]{0,1:T(8,128)(2,1)}, bf16[256,512]{0,1:T(8,128)(2,1)}, u32[]{:S(2)}, u32[]{:S(2)}) collective-permute-start(bf16[256,512]{0,1:T(8,128)(2,1)} %pad_maximum_fusion.9), channel_id=1, source_target_pairs={{1,0},{2,1},{3,2},{4,3},{5,4},{6,5},{7,6},{8,7},{9,8},{10,9},{11,1... | collective-permute-start | bytes 786440 | tf_op jit(solution)/shard_map/ppermute | solution.py:39
  21.8 29.5 %collective-permute-start = (bf16[256,512]{0,1:T(8,128)(2,1)}, bf16[256,512]{0,1:T(8,128)(2,1)}, u32[]{:S(2)}, u32[]{:S(2)}) collective-permute-start(bf16[256,512]{0,1:T(8,128)(2,1)} %pad_maximum_fusion.9), channel_id=1, source_target_pairs={{0,1},{1,2},{2,3},{3,4},{4,5},{5,6},{6,7},{7,8},{8,9},{9,10},{10,1... | collective-permute-start | bytes 786440 | tf_op jit(solution)/shard_map/ppermute | solution.py:38
  30.3 294.3 %reduce-scatter.8.cloned.1.call-start = ((), (), s32[]{:S(2)}) async-start(), calls=%async_computation.6 | async-start | bytes 2621440 | tf_op jit(solution)/shard_map/reduce_scatter | solution.py:237
  84.7 476.0 %reduce-scatter.10.cloned.1.call-start = ((), (), s32[]{:S(2)}) async-start(), calls=%async_computation.7 | async-start | bytes 2162688
  135.4 8.7 copy-start.66
  135.5 8.7 copy-start.67
  135.5 8.7 copy-start.68
  135.5 8.7 copy-start.69
  135.5 8.7 copy-start.70
  135.5 8.7 copy-start.71
  135.5 8.7 copy-start.72
  135.5 8.7 copy-start.73
  135.5 8.7 copy-start.74
  135.5 8.7 copy-start.75
  135.5 8.7 copy-start.76
  135.6 8.7 copy-start.77
  135.6 8.7 copy-start.78
  135.6 8.7 copy-start.79
  135.7 112.7 %copy-start.58 = (f32[2,256]{1,0:T(2,128)S(1)}, f32[2,256]{1,0:T(2,128)}, u32[]{:S(2)}) copy-start(f32[2,256]{1,0:T(2,128)} %copy-done.57) | copy-start | bytes 6148
  136.6 117.0 %collective-permute-start.4 = (bf16[256,512]{0,1:T(8,128)(2,1)}, bf16[256,512]{0,1:T(8,128)(2,1)}, u32[]{:S(2)}, u32[]{:S(2)}) collective-permute-start(bf16[256,512]{0,1:T(8,128)(2,1)} %get-tuple-element.444), channel_id=1, source_target_pairs={{1,0},{2,1},{3,2},{4,3},{5,4},{6,5},{7,6},{8,7},{9,8},{10,9},{11,1... | collective-permute-start | bytes 786440 | tf_op jit(solution)/shard_map/ppermute | solution.py:28
  137.9 115.7 %collective-permute-start.5 = (bf16[256,512]{0,1:T(8,128)(2,1)}, bf16[256,512]{0,1:T(8,128)(2,1)}, u32[]{:S(2)}, u32[]{:S(2)}) collective-permute-start(bf16[256,512]{0,1:T(8,128)(2,1)} %get-tuple-element.445), channel_id=1, source_target_pairs={{0,1},{1,2},{2,3},{3,4},{4,5},{5,6},{6,7},{7,8},{8,9},{9,10},{10,1... | collective-permute-start | bytes 786440 | tf_op jit(solution)/shard_map/ppermute | solution.py:28
  265.0 1055.0 %reduce-scatter.12.cloned.1.call-start = ((), (), s32[]{:S(2)}) async-start(), calls=%async_computation.8 | async-start | bytes 2113536 | tf_op jit(solution)/shard_map/reduce_scatter | solution.py:237
  267.5 9.2 copy-start.33
  561.8 759.4 %copy-start.38 = (bf16[256,256]{0,1:T(8,128)(2,1)S(1)}, bf16[256,256]{0,1:T(8,128)(2,1)}, u32[]{:S(2)}) copy-start(bf16[256,256]{0,1:T(8,128)(2,1)} %get-tuple-element.482) | copy-start | bytes 393220
  (104 other events, 522.6 us)
Sparse Core Ops, SparseCore 0:
  10.7 59.6 all-gather.3
  73.6 80.2 all-gather.5
  158.3 117.0 all-gather.7
  278.1 46.4 reduce-scatter.7
  329.6 231.0 reduce-scatter.9
  563.3 756.6 reduce-scatter.11
where the time goes:
time: 1330 us
  waiting for transfers between devices  1050 us (79%)
  blocking collectives  103 us (8%)
  local copies, waits for them, and re-layouts  80.6 us (6%)
  matrix products  32.6 us (2%)
  other arithmetic  26.9 us (2%)
  starting transfers between devices  24.9 us (2%)
  between operations  16.5 us (1%)
    reduce_scatter x2, waiting for transfers between devices, dilated(): own = lax.psum_scatter(partial_sums, bits, scatter_dimension=0, tiled=True)  796 us
    unnamed x7, waiting for transfers between devices  234 us
    psum x1, blocking collectives, shards(): bias_grad = lax.psum(band[4], ('dp',) + CTX)  103 us
    another operation x33, local copies, waits for them, and re-layouts, bucket_sums(): return jnp.stack(totals, axis=0)  41.6 us
  transfers between devices with their start and end apart: 12, of which 6 were waited for; matrix products, arithmetic and copies ran while one was open for 10% of the time, Pallas kernels for 0%

commit v1 on v0

--- a/solution.py
+++ b/solution.py
@@ -10,6 +10,11 @@
 DILATION_SECOND = 8
 DILATION_THIRD = 32
 CTX = ("cx", "cy", "cz")
+
+
+def add_all(array, axis):
+    terms = lax.all_gather(array, axis)
+    return jnp.sum(terms, axis=0)
 
 
 def swapped(block, axis, bit):
@@ -275,7 +280,7 @@
                 score_scale,
             )
         )
-    bias_grad = lax.psum(band[4], ("dp",) + CTX)
+    bias_grad = add_all(band[4], ("dp",) + CTX)
     joined = [
         jnp.concatenate([piece[slot] for piece in pieces], axis=1)
         .reshape(1, rows, width)

time: 1330 us -> 2700 us (2.03)
  blocking collectives: 103 us -> 1550 us
  waiting for transfers between devices: 1050 us -> 965 us
    all_gather x0 -> x1, blocking collectives: none -> 1550 us  [add_all(): terms = lax.all_gather(array, axis)]
    psum x1 -> x0, blocking collectives: 103 us -> none  [shards(): bias_grad = lax.psum(band[4], ('dp',) + CTX)]
    reduce_scatter x2, waiting for transfers between devices: 796 us -> 757 us  [dilated(): own = lax.psum_scatter(partial_sums, bits, scatter_dimension=0, tiled=True)]
    unnamed x7, waiting for transfers between devices: 234 us -> 201 us
  transfers between devices with their start and end apart: 12 -> 12, of which waited for: 6 -> 4; matrix products, arithmetic and copies ran while one was open for 10% -> 5% of each run, Pallas kernels for 0% -> 0%
where the time goes in v1:
time: 2700 us
  blocking collectives  1550 us (57%)
  waiting for transfers between devices  965 us (36%)
  local copies, waits for them, and re-layouts  83.1 us (3%)
  matrix products  32.3 us (1%)
  other arithmetic  30.7 us (1%)
    all_gather x1, blocking collectives, add_all(): terms = lax.all_gather(array, axis)  1550 us
    reduce_scatter x2, waiting for transfers between devices, dilated(): own = lax.psum_scatter(partial_sums, bits, scatter_dimension=0, tiled=True)  757 us
    unnamed x7, waiting for transfers between devices  201 us
  transfers between devices with their start and end apart: 12, of which 4 were waited for; matrix products, arithmetic and copies ran while one was open for 5% of the time, Pallas kernels for 0%

profile of v1, /device:TPU:64, one launch (start us, length us, event | category | flops | bytes accessed | tf_op | source)
XLA Modules:
  0.0 2702.0 jit_solution(6241908919485350767)
XLA Ops:
  13.8 6.7 collective-permute-start.2
  22.6 7.8 collective-permute-start
  35.6 1.4 fusion.55
  42.1 5.3 fusion.53
  47.9 4.2 collective-permute-done
  53.8 5.7 fusion.9
  61.1 5.6 select_reduce_fusion
  66.7 3.3 all-gather.6.cloned.1.call-done
  71.3 3.7 fusion.132
  75.1 3.2 fusion.60
  78.3 2.3 multiply_reduce_fusion
  82.7 1.5 pad_maximum_fusion
  84.3 5.4 select_reduce_fusion.18
  99.9 1.3 copy.596
  103.8 1.3 copy.593
  106.4 1.3 copy.591
  109.0 1.3 copy.589
  114.1 1.3 copy.585
  117.9 1.3 copy.580
  130.7 3.4 fusion.65
  137.7 6.2 collective-permute-start.5
  145.0 1549.5 %all-gather.1 = f32[512,32,2]{1,2,0:T(2,128)} all-gather(f32[1,32,2]{1,2,0:T(2,128)S(1)} %bitcast.410), channel_id=2, replica_groups=mesh['dp'=4,'cx'=4,'cy'=8,'cz'=4] {'dp','cx','cy','cz'}, dimensions={0}, use_global_device_ids=true | all-gather | bytes 131328 | tf_op jit(solution)/shard_map/all_gather | solution.py:16
  1694.5 2.2 reduce_sum.409
  1696.6 3.2 fusion.15
  1699.8 2.0 fusion.16
  1703.8 2.0 convolution_bitcast_fusion
  1710.5 1.5 pad_maximum_fusion.1
  1712.0 2.9 copy.629
  1721.8 1.3 fusion.77
  1724.5 1.9 copy.631
  1732.6 200.8 %reduce-scatter.10.cloned.1.call-done = f32[32,512]{1,0:T(8,128)} async-done(((f32[1024,512]{1,0:T(8,128)}), f32[32,512]{1,0:T(8,128)}) %reduce-scatter.10.cloned.1.call-update) | async-done | bytes 65552
  1935.2 756.6 %reduce-scatter.12.cloned.1.call-done = f32[8,512]{1,0:T(8,128)} async-done(((f32[1024,512]{1,0:T(8,128)}), f32[8,512]{1,0:T(8,128)}) %reduce-scatter.12.cloned.1.call-update) | async-done | bytes 16400 | tf_op jit(solution)/shard_map/reduce_scatter | solution.py:242
  (442 shorter events, 88.0 us)
Async XLA Ops:
  7.2 62.9 %all-gather.6.cloned.1.call-start = ((), (), s32[]{:S(2)}) async-start(), calls=%async_computation.3 | async-start | bytes 1310720 | tf_op jit(solution)/shard_map/all_gather | solution.py:220
  10.6 1695.2 %all-gather.8.cloned.1.call-start = ((), (), s32[]{:S(2)}) async-start(), calls=%async_computation.4 | async-start | bytes 1081344 | tf_op jit(solution)/shard_map/all_gather | solution.py:220
  10.7 21.2 copy-start.13
  10.8 22.2 copy-start.6
  12.5 1706.4 %all-gather.10.cloned.1.call-start = ((), (), s32[]{:S(2)}) async-start(), calls=%async_computation.5 | async-start | bytes 1056768 | tf_op jit(solution)/shard_map/all_gather | solution.py:220
  12.5 29.6 %collective-permute-start.3 = (s32[256]{0:T(256)S(1)}, s32[256]{0:T(256)S(1)}, u32[]{:S(2)}, u32[]{:S(2)}) collective-permute-start(s32[256]{0:T(256)S(1)} %bitcast.407), channel_id=1, source_target_pairs={{1,0},{2,1},{3,2},{4,3},{5,4},{6,5},{7,6},{8,7},{9,8},{10,9},{11,1... | collective-permute-start | bytes 3080 | tf_op jit(solution)/shard_map/ppermute | solution.py:44
  13.8 28.3 %collective-permute-start.2 = (s32[256]{0:T(256)S(1)}, s32[256]{0:T(256)S(1)}, u32[]{:S(2)}, u32[]{:S(2)}) collective-permute-start(s32[256]{0:T(256)S(1)} %bitcast.408), channel_id=1, source_target_pairs={{0,1},{1,2},{2,3},{3,4},{4,5},{5,6},{6,7},{7,8},{8,9},{9,10},{10,1... | collective-permute-start | bytes 3080 | tf_op jit(solution)/shard_map/ppermute | solution.py:43
  20.6 12.8 copy-start.7
  21.3 26.6 collective-permute-start.1
  22.6 29.6 %collective-permute-start = (bf16[256,512]{0,1:T(8,128)(2,1)}, bf16[256,512]{0,1:T(8,128)(2,1)}, u32[]{:S(2)}, u32[]{:S(2)}) collective-permute-start(bf16[256,512]{0,1:T(8,128)(2,1)} %pad_maximum_fusion.9), channel_id=1, source_target_pairs={{0,1},{1,2},{2,3},{3,4},{4,5},{5,6},{6,7},{7,8},{8,9},{9,10},{10,1... | collective-permute-start | bytes 786440 | tf_op jit(solution)/shard_map/ppermute | solution.py:43
  31.8 1698.3 %reduce-scatter.8.cloned.1.call-start = ((), (), s32[]{:S(2)}) async-start(), calls=%async_computation.6 | async-start | bytes 2621440 | tf_op jit(solution)/shard_map/reduce_scatter | solution.py:242
  84.3 1849.1 %reduce-scatter.10.cloned.1.call-start = ((), (), s32[]{:S(2)}) async-start(), calls=%async_computation.7 | async-start | bytes 2162688
  135.2 8.7 copy-start.62
  135.2 8.7 copy-start.63
  135.2 8.7 copy-start.64
  135.2 8.7 copy-start.65
  135.2 8.7 copy-start.66
  135.3 8.7 copy-start.67
  135.3 8.7 copy-start.68
  135.3 8.7 copy-start.69
  135.3 8.7 copy-start.70
  135.3 8.7 copy-start.71
  135.3 8.7 copy-start.72
  135.3 8.7 copy-start.73
  135.3 8.7 copy-start.74
  135.3 8.7 copy-start.75
  135.3 8.7 copy-start.76
  135.6 1561.1 %copy-start.54 = (f32[2,256]{1,0:T(2,128)S(1)}, f32[2,256]{1,0:T(2,128)}, u32[]{:S(2)}) copy-start(f32[2,256]{1,0:T(2,128)} %copy-done.53) | copy-start | bytes 6148
  136.4 1565.4 %collective-permute-start.4 = (bf16[256,512]{0,1:T(8,128)(2,1)}, bf16[256,512]{0,1:T(8,128)(2,1)}, u32[]{:S(2)}, u32[]{:S(2)}) collective-permute-start(bf16[256,512]{0,1:T(8,128)(2,1)} %get-tuple-element.444), channel_id=1, source_target_pairs={{1,0},{2,1},{3,2},{4,3},{5,4},{6,5},{7,6},{8,7},{9,8},{10,9},{11,1... | collective-permute-start | bytes 786440 | tf_op jit(solution)/shard_map/ppermute | solution.py:33
  137.7 1564.2 %collective-permute-start.5 = (bf16[256,512]{0,1:T(8,128)(2,1)}, bf16[256,512]{0,1:T(8,128)(2,1)}, u32[]{:S(2)}, u32[]{:S(2)}) collective-permute-start(bf16[256,512]{0,1:T(8,128)(2,1)} %get-tuple-element.445), channel_id=1, source_target_pairs={{0,1},{1,2},{2,3},{3,4},{4,5},{5,6},{6,7},{7,8},{8,9},{9,10},{10,1... | collective-permute-start | bytes 786440 | tf_op jit(solution)/shard_map/ppermute | solution.py:33
  1715.0 976.8 %reduce-scatter.12.cloned.1.call-start = ((), (), s32[]{:S(2)}) async-start(), calls=%async_computation.8 | async-start | bytes 2113536 | tf_op jit(solution)/shard_map/reduce_scatter | solution.py:242
  1934.5 758.5 %copy-start.34 = (bf16[256,256]{0,1:T(8,128)(2,1)S(1)}, bf16[256,256]{0,1:T(8,128)(2,1)}, u32[]{:S(2)}) copy-start(bf16[256,256]{0,1:T(8,128)(2,1)} %get-tuple-element.482) | copy-start | bytes 393220
  (100 other events, 468.9 us)
Sparse Core Ops, SparseCore 0:
  10.7 59.2 all-gather.5
  73.2 79.1 all-gather.7
  156.8 111.4 all-gather.9
  271.0 46.6 reduce-scatter.7
  1715.1 218.2 reduce-scatter.9
  1936.0 755.7 reduce-scatter.11
